TPU v7x, 32 devices: a whole 2x2x4 slice. The times are simulated.
32 devices in a mesh: day: 4 (over z), dom: 8 (over y, x, core).
Axes of the slice: x: 2, y: 2, z: 4, core: 2. Of those that a mesh axis runs over, the one named last changes fastest.
Arguments:
- node_states: bfloat16 [16, 2048, 256], P('day', 'dom'), may hold values from -12 to 12
- edge_source: int32 [16, 8192], P('day', 'dom'), may hold values from 0 to 383
- edge_target: int32 [16, 8192], P('day', 'dom'), may hold values from 0 to 255
- halo_rows: int32 [16, 1024], P('day', 'dom'), may hold values from 0 to 255
- halo_count: int32 [16, 8], P('day', 'dom'), may hold values from 1 to 128, 640 in all within a row
- w_message: bfloat16 [256, 256], replicated, may hold values from -0.375 to 0.375
- w_query: bfloat16 [256, 256], replicated, may hold values from -1 to 1, as said below
- w_key: bfloat16 [256, 256], replicated, may hold values from -1 to 1, as said below
- w_value: bfloat16 [256, 256], replicated, may hold values from -0.375 to 0.375
- cotangent: bfloat16 [16, 8, 4, 64, 256], P(None, 'dom', 'day'), may hold values from -6 to 6
Outputs:
- state_grad: float32 [16, 2048, 256], P('day', 'dom')
- grad_message: float32 [256, 256], replicated
- grad_query: float32 [256, 256], replicated
- grad_key: float32 [256, 256], replicated
- grad_value: float32 [256, 256], replicated
Inputs may be any that keep to these rules, and one draw needn't show every extreme that they name: `edge_source`: indices of the extended rows: below 256 a partition's own account, from 256 on a received halo slot. `halo_rows`: rows of the sending partition's own block; repeats allowed. `halo_count`: on every day some partition has all 128 slots live. `w_query`: entries of order 256 ** -0.5. `w_key`: entries of order 256 ** -0.5.
All inputs are finite; a program needn't handle non-finite values. No bound on the sum of `halo_count` on one device may be relied on, other than what follows from the above.
Results may differ from a plain program's by a relative error of at most 0.004.
The roundings to bfloat16 on the way count: a program that leaves them out, or rounds other values in their place, can miss the bound.
Values may be sent and summed in bfloat16 or wider, within the bound.
No kernel may reach another device: no remote copies, remote signals or barrier semaphores. Data moves between devices by JAX's collectives and lax.ppermute only.
A program may use at most 64 MiB of HBM per device.

v0:
```python
import jax
import jax.numpy as jnp
from jax import lax
from jax.sharding import PartitionSpec as P

HEADS = 4


def from_behind(value, axis, steps):
    count = lax.axis_size(axis)
    pairs = [(source, (source + steps) % count) for source in range(count)]
    return lax.ppermute(value, axis, pairs)


def adjacency(sources, targets, count_rows, total_rows):
    target_hot = (targets[:, None] == jnp.arange(count_rows, dtype=jnp.int32)[None, :]).astype(
        jnp.bfloat16
    )
    source_hot = (sources[:, None] == jnp.arange(total_rows, dtype=jnp.int32)[None, :]).astype(
        jnp.bfloat16
    )
    counts = lax.dot_general(
        target_hot, source_hot, (((0,), (0,)), ((), ())), preferred_element_type=jnp.float32
    )
    return counts.astype(jnp.bfloat16)


def gnn_forward(states, received, adjacent, w_message):
    extended = jnp.concatenate([states, received], axis=0)
    neighbours = jnp.dot(adjacent, extended, preferred_element_type=jnp.float32)
    counted = jnp.sum(adjacent.astype(jnp.float32), axis=1)
    inverse = 1.0 / (counted + 1.0)
    aggregate = ((states.astype(jnp.float32) + neighbours) * inverse[:, None]).astype(jnp.bfloat16)
    preact = jnp.dot(aggregate, w_message, preferred_element_type=jnp.float32)
    hidden = (states.astype(jnp.float32) + jax.nn.silu(preact)).astype(jnp.bfloat16)
    return (aggregate, preact, inverse, hidden)


def gnn_backward(upstream, aggregate, preact, inverse, adjacent, w_message):
    count_rows = aggregate.shape[0]
    up_float = upstream.astype(jnp.float32)
    sigmoid_val = jax.nn.sigmoid(preact)
    pre_grad = (up_float * sigmoid_val * (1.0 + preact * (1.0 - sigmoid_val))).astype(jnp.bfloat16)
    message_part = lax.dot_general(
        aggregate, pre_grad, (((0,), (0,)), ((), ())), preferred_element_type=jnp.float32
    )
    agg_grad = lax.dot_general(
        pre_grad, w_message, (((1,), (1,)), ((), ())), preferred_element_type=jnp.float32
    )
    term_grad = agg_grad * inverse[:, None]
    ext_grad = lax.dot_general(
        adjacent.astype(jnp.float32),
        term_grad,
        (((0,), (0,)), ((), ())),
        precision=lax.Precision.HIGHEST,
        preferred_element_type=jnp.float32,
    )
    local_grad = up_float + term_grad + ext_grad[:count_rows]
    halo_grad = ext_grad[count_rows:].astype(jnp.bfloat16)
    return (message_part, local_grad, halo_grad)


def attend(states, upstream, w_query, w_key, w_value):
    steps_all, nodes_here, width = states.shape
    head_dim = width // HEADS
    scale_factor = head_dim ** (-0.5)
    flat = states.reshape(steps_all * nodes_here, width)

    def project(weight):
        return jnp.dot(flat, weight, preferred_element_type=jnp.float32).astype(jnp.bfloat16)

    def splitter(matrix):
        return matrix.reshape(steps_all, nodes_here, HEADS, head_dim).astype(jnp.float32)

    queries = project(w_query)
    key_rows = project(w_key)
    value_rows = project(w_value)
    query_f = splitter(queries)
    key_f = splitter(key_rows)
    value_f = splitter(value_rows)
    scores = jnp.einsum("tnhd,snhd->nhts", query_f, key_f) * scale_factor
    causal = jnp.arange(steps_all)[:, None] >= jnp.arange(steps_all)[None, :]
    scores = jnp.where(causal, scores, -jnp.inf)
    highest = jnp.max(scores, axis=-1, keepdims=True)
    exponent = jnp.exp(scores - highest)
    probs = exponent / jnp.sum(exponent, axis=-1, keepdims=True)
    probs_low = probs.astype(jnp.bfloat16).astype(jnp.float32)
    up_heads = splitter(upstream)
    value_grad = jnp.einsum("nhts,tnhd->snhd", probs_low, up_heads).astype(jnp.bfloat16)
    prob_grad = jnp.einsum("tnhd,snhd->nhts", up_heads, value_f)
    score_grad = (
        probs * (prob_grad - jnp.sum(prob_grad * probs, axis=-1, keepdims=True)) * scale_factor
    ).astype(jnp.bfloat16)
    score_f = score_grad.astype(jnp.float32)
    query_grad = jnp.einsum("nhts,snhd->tnhd", score_f, key_f).astype(jnp.bfloat16)
    key_grad = jnp.einsum("nhts,tnhd->snhd", score_f, query_f).astype(jnp.bfloat16)
    query_flat = query_grad.reshape(steps_all * nodes_here, width)
    key_flat = key_grad.reshape(steps_all * nodes_here, width)
    value_flat = value_grad.reshape(steps_all * nodes_here, width)

    def weight_grad(grad_rows):
        return lax.dot_general(
            flat, grad_rows, (((0,), (0,)), ((), ())), preferred_element_type=jnp.float32
        )

    def input_grad(grad_rows, weight):
        return lax.dot_general(
            grad_rows, weight, (((1,), (1,)), ((), ())), preferred_element_type=jnp.float32
        )

    back = upstream.reshape(steps_all * nodes_here, width).astype(jnp.float32)
    back = (
        back
        + input_grad(query_flat, w_query)
        + input_grad(key_flat, w_key)
        + input_grad(value_flat, w_value)
    )
    back = back.astype(jnp.bfloat16).reshape(steps_all, nodes_here, width)
    return ((weight_grad(query_flat), weight_grad(key_flat), weight_grad(value_flat)), back)


def local(
    node_states,
    edge_source,
    edge_target,
    halo_rows,
    halo_count,
    w_message,
    w_query,
    w_key,
    w_value,
    cotangent,
):
    days_local, node_local, width = node_states.shape
    halo_slots = halo_rows.shape[1]
    live = jnp.arange(halo_slots)[None, :] < halo_count
    picked = jnp.take_along_axis(node_states, halo_rows[:, :, None], axis=1)
    sent = jnp.where(live[:, :, None], picked, jnp.zeros_like(picked))
    received = from_behind(sent, "dom", 1)

    def forward_one(items):
        adjacent = adjacency(items[2], items[3], node_local, node_local + halo_slots)
        aggregate, preact, inverse, hidden = gnn_forward(items[0], items[1], adjacent, w_message)
        return (aggregate, preact, inverse, hidden, adjacent)

    aggregate, preact, inverse, hidden, adjacent = lax.map(
        forward_one, (node_states, received, edge_source, edge_target)
    )
    node_major = lax.all_to_all(hidden, "day", split_axis=1, concat_axis=0, tiled=True)
    upstream = cotangent.reshape(cotangent.shape[0], -1, width)
    attn_grads, back = attend(node_major, upstream, w_query, w_key, w_value)
    back_days = lax.all_to_all(back, "day", split_axis=0, concat_axis=1, tiled=True)

    def backward_one(items):
        return gnn_backward(items[0], items[1], items[2], items[3], items[4], w_message)

    message_parts, local_grad, halo_grad = lax.map(
        backward_one, (back_days, aggregate, preact, inverse, adjacent)
    )
    grad_message = jnp.sum(message_parts, axis=0)
    returned = from_behind(halo_grad, "dom", -1)
    slot_hot = jnp.logical_and(
        halo_rows[:, :, None] == jnp.arange(node_local, dtype=jnp.int32)[None, None, :],
        live[:, :, None],
    ).astype(jnp.bfloat16)
    scattered = jnp.einsum("dsn,dsh->dnh", slot_hot, returned, preferred_element_type=jnp.float32)
    state_grad = local_grad + scattered
    grad_message, grad_query, grad_key, grad_value = lax.psum(
        (grad_message, attn_grads[0], attn_grads[1], attn_grads[2]), ("day", "dom")
    )
    return (state_grad, grad_message, grad_query, grad_key, grad_value)


def solution(mesh):
    return jax.shard_map(
        local,
        mesh=mesh,
        in_specs=(
            P("day", "dom", None),
            P("day", "dom"),
            P("day", "dom"),
            P("day", "dom"),
            P("day", "dom"),
            P(),
            P(),
            P(),
            P(),
            P(None, "dom", "day", None, None),
        ),
        out_specs=(P("day", "dom", None), P(), P(), P(), P()),
        check_vma=False,
    )
```

profile of v0, /device:TPU:0, one launch (start us, length us, event | category | flops | bytes accessed | tf_op | source)
XLA Modules:
  0.0 277.3 jit_solution(9602864403409959612)
XLA Ops:
  7.2 0.7 fusion.70
  7.9 0.8 iota_compare_fusion.8
  8.7 7.0 %gather_fusion = bf16[512,256]{1,0:T(8,128)(2,1)S(1)} fusion(bf16[4,256,256]{2,1,0:T(8,128)(2,1)} %param.14, s32[512]{0:T(512)S(1)} %fusion.70), kind=kCustom, calls=%fused_computation | custom fusion | bytes 528384 | tf_op jit(solution)/shard_map/jit(take_along_axis)/gather | solution.py:137
  16.4 6.9 %collective-permute-done = bf16[4,128,256]{2,1,0:T(8,128)(2,1)S(1)} collective-permute-done((bf16[4,128,256]{2,1,0:T(8,128)(2,1)S(1)}, bf16[4,128,256]{2,1,0:T(8,128)(2,1)S(1)}, u32[]{:S(2)}, u32[]{:S(2)}) %collective-permute-start) | collective-permute-done | bytes 262176 | tf_op jit(solution)/shard_map/ppermute | solution.py:12
  23.4 12.2 %while.34 = (s32[]{:T(128)}, bf16[4,256,256]{2,1,0:T(8,128)(2,1)S(1)}, f32[4,256,256]{2,1,0:T(8,128)S(1)}, f32[4,256]{1,0:T(4,128)S(1)}, bf16[4,256,256]{2,1,0:T...) while((s32[]{:T(128)}, ...), condition=%wide.region_2.3_spmd.clone, body=%wide.region_0.2_spmd.sunk.clone | while | flops 287277312 | bytes 3111561 | solution.py:146
  23.5 0.7 constant_dynamic-slice_fusion.7
  24.2 1.0 convert_reduce_fusion.3
  25.8 0.7 bitcast_dynamic-update-slice_fusion.15
  26.5 0.7 constant_dynamic-slice_fusion.7
  27.3 1.0 convert_reduce_fusion.3
  28.8 0.7 bitcast_dynamic-update-slice_fusion.15
  29.5 0.7 constant_dynamic-slice_fusion.7
  30.3 1.0 convert_reduce_fusion.3
  31.8 0.7 bitcast_dynamic-update-slice_fusion.15
  32.6 0.7 constant_dynamic-slice_fusion.7
  33.3 1.0 convert_reduce_fusion.3
  34.9 0.7 bitcast_dynamic-update-slice_fusion.15
  35.6 1.2 copy.52
  36.9 5.6 %all-to-all-start = ((bf16[4,256,256]{2,0,1:T(4,128)(2,1)}), bf16[4,256,256]{2,0,1:T(4,128)(2,1)S(1)}, u32[]{:S(2)}, u32[]{:S(2)}) async-start(bf16[4,256,256]{2,0,1:T(4,128)(2,1)} %copy.52), calls=%async_computation | async-start | bytes 1048576 | tf_op jit(solution)/shard_map/all_to_all | solution.py:149
  42.9 12.5 %all-to-all-done = bf16[4,256,256]{2,0,1:T(4,128)(2,1)S(1)} async-done(((bf16[4,256,256]{2,0,1:T(4,128)(2,1)}), bf16[4,256,256]{2,0,1:T(4,128)(2,1)S(1)}, u32[]{:S(2)}, u32[]{:S(2)}) %all-to-all-start) | async-done | bytes 524320 | tf_op jit(solution)/shard_map/all_to_all | solution.py:149
  55.8 1.4 reshape.100
  57.5 1.4 reshape.99
  59.6 2.6 fusion.52
  62.3 4.9 %fusion.77 = (f32[64,4,16]{2,1,0:T(4,128)S(1)}, f32[64,4,16,16]{2,3,1,0:T(8,128)}) fusion(pred[16,16]{0,1:T(8,128)(4,1)S(1)} %iota_compare_fusion.7, bf16[16,64,4,64]{3,2,1,0:T(4,128)(2,1)} %reshape.99, bf16[16,64,4,64]{3,2,1,0:T(4,128)(2,1)} %reshape.100), kind=kOutput, calls=%fused_computation.119 | convolution fusion | flops 8650767 | bytes 1327360 | tf_op jit(solution)/shard_map/sub | solution.py:85
  67.2 5.8 %fusion.50 = bf16[16,64,4,64]{3,0,2,1:T(8,128)(2,1)} fusion(f32[64,4,16,16]{3,2,1,0:T(8,128)} %fusion.52, bf16[16,64,4,64]{3,2,1,0:T(4,128)(2,1)S(1)} %copy-done.5, f32[64,4,16,16]{2,3,1,0:T(8,128)} %get-tuple-element.183, f32[64,4,16]{2,1,0:T(4,128)S(1)} %get-tuple-element.182), kind=kOutput, calls=%fused_computation.78 | convolution fusion | flops 9113615 | bytes 1589248 | tf_op jit(solution)/shard_map/nhts,tnhd->snhd/dot_general | solution.py:96
  73.0 6.1 %fusion.48 = bf16[16,64,4,64]{3,0,2,1:T(8,128)(2,1)} fusion(f32[64,4,16,16]{3,2,1,0:T(8,128)} %fusion.52, bf16[16,64,4,64]{3,2,1,0:T(4,128)(2,1)} %reshape.99, f32[64,4,16,16]{2,3,1,0:T(8,128)} %get-tuple-element.183, f32[64,4,16]{2,1,0:T(4,128)S(1)} %get-tuple-element.182), kind=kOutput, calls=%fused_computation.76 | convolution fusion | flops 9113615 | bytes 1589248 | tf_op jit(solution)/shard_map/nhts,snhd->tnhd/dot_general | solution.py:95
  79.2 3.5 %fusion.49 = bf16[16,64,4,64]{3,0,2,1:T(8,128)(2,1)} fusion(bf16[16,64,4,64]{3,2,1,0:T(4,128)(2,1)S(1)} %reshape_reshape.4, f32[64,4,16,16]{2,3,1,0:T(8,128)} %get-tuple-element.183, f32[64,4,16]{2,1,0:T(4,128)} %copy-done.13), kind=kOutput, calls=%fused_computation.77 | convolution fusion | flops 8781824 | bytes 1327104 | tf_op jit(solution)/shard_map/nhts,tnhd->snhd/dot_general | solution.py:89
  82.7 1.7 copy.63
  84.4 0.7 reshape.103
  85.2 3.1 %copy.61 = bf16[16,64,4,64]{1,0,3,2:T(8,128)(2,1)S(1)} copy(bf16[16,64,4,64]{3,0,2,1:T(8,128)(2,1)} %fusion.48) | data formatting | bytes 1048576 | tf_op jit(solution)/shard_map/convert_element_type | solution.py:95
  88.3 0.7 reshape.102
  89.0 2.9 %copy.65 = bf16[16,64,4,64]{1,0,3,2:T(8,128)(2,1)S(1)} copy(bf16[16,64,4,64]{3,0,2,1:T(8,128)(2,1)} %fusion.49) | data formatting | bytes 1048576 | tf_op jit(solution)/shard_map/convert_element_type | solution.py:89
  91.9 0.7 reshape.104
  92.7 1.4 convolution_add_fusion.3
  94.5 1.2 fusion.51
  95.6 3.5 %all-to-all-start.1 = ((bf16[16,64,256]{2,1,0:T(8,128)(2,1)}), bf16[16,64,256]{2,1,0:T(8,128)(2,1)S(1)}, u32[]{:S(2)}, u32[]{:S(2)}) async-start(bf16[16,64,256]{2,1,0:T(8,128)(2,1)} %bitcast.30), calls=%async_computation.1 | async-start | bytes 1048576 | tf_op jit(solution)/shard_map/all_to_all | solution.py:152
  99.2 1.0 fusion.87
  100.2 1.0 fusion.86
  101.3 10.9 %all-to-all-done.1 = bf16[16,64,256]{2,1,0:T(8,128)(2,1)S(1)} async-done(((bf16[16,64,256]{2,1,0:T(8,128)(2,1)}), bf16[16,64,256]{2,1,0:T(8,128)(2,1)S(1)}, u32[]{:S(2)}, u32[]{:S(2)}) %all-to-all-start.1) | async-done | bytes 524320 | tf_op jit(solution)/shard_map/all_to_all | solution.py:152
  112.1 0.8 copy.66
  113.1 18.6 %while.35 = (s32[]{:T(128)}, f32[4,256,256]{2,1,0:T(8,128)S(1)}, f32[4,256,256]{2,1,0:T(8,128)S(1)}, bf16[4,128,256]{2,1,0:T(8,128)(2,1)}, bf16[4,256,256]{2,1,0...) while((s32[]{:T(128)}, f32[4,256,256]{2,1,0:T(8,128)S(1)}, ...), condition=%wide.region_7.8_spmd.clone, body=%wide.region_6.7_spmd.sunk.clone | while | flops 370671616 | bytes 5576841 | solution.py:157
  113.2 1.3 convolution_multiply_fusion.3
  114.5 1.3 fusion.149
  115.8 0.6 fusion.151
  116.5 1.3 fusion.148
  117.8 1.3 convolution_multiply_fusion.3
  119.1 1.3 fusion.149
  120.5 0.6 fusion.151
  121.1 1.3 fusion.148
  122.5 1.3 convolution_multiply_fusion.3
  123.8 1.3 fusion.149
  125.8 1.3 fusion.148
  127.1 1.3 convolution_multiply_fusion.3
  128.4 1.3 fusion.149
  130.4 1.3 fusion.148
  131.8 1.1 fusion.88
  132.9 0.8 reduce_sum.38
  133.7 2.3 collective-permute-done.1
  136.0 2.4 convolution_add_fusion.4
  138.5 125.3 %all-reduce.3.cloned.1.call-done = (f32[256,256]{1,0:T(8,128)}, f32[256,256]{1,0:T(8,128)}, f32[256,256]{1,0:T(8,128)}, f32[256,256]{1,0:T(8,128)}) async-done(((f32[256,256]{1,0:T(8,128)}, f32[256,256]{1,0:T(8,128)}, f32[256,256]{1,0:T(8,128)}, f32[256,256]{1,0:T(8,128)}), (f32[256,256]{1,0:T(8,128)}, f32[256,256]{1,0:T(8,128)}, f32[256,256]{1,0:T(8,128)}, ...) | async-done | bytes 1048592 | tf_op jit(solution)/shard_map/psum | solution.py:168
  263.8 1.7 copy.137
  265.5 1.7 copy.138
  267.1 1.7 copy.139
  268.8 1.7 copy.140
  (94 shorter events, 7.1 us)
Async XLA Ops:
  7.2 48.3 %copy-start = (bf16[256,256]{1,0:T(8,128)(2,1)S(1)}, bf16[256,256]{1,0:T(8,128)(2,1)}, u32[]{:S(2)}) copy-start(bf16[256,256]{1,0:T(8,128)(2,1)} %param.20) | copy-start | bytes 393220
  8.7 14.8 %copy-start.1 = (bf16[4,256,256]{2,1,0:T(8,128)(2,1)S(1)}, bf16[4,256,256]{2,1,0:T(8,128)(2,1)}, u32[]{:S(2)}) copy-start(bf16[4,256,256]{2,1,0:T(8,128)(2,1)} %param.14) | copy-start | bytes 1572868
  8.7 14.8 %copy-start.2 = (bf16[256,256]{1,0:T(8,128)(2,1)S(1)}, bf16[256,256]{1,0:T(8,128)(2,1)}, u32[]{:S(2)}) copy-start(bf16[256,256]{1,0:T(8,128)(2,1)} %param.19) | copy-start | bytes 393220
  15.9 7.4 %collective-permute-start = (bf16[4,128,256]{2,1,0:T(8,128)(2,1)S(1)}, bf16[4,128,256]{2,1,0:T(8,128)(2,1)S(1)}, u32[]{:S(2)}, u32[]{:S(2)}) collective-permute-start(bf16[4,128,256]{2,1,0:T(8,128)(2,1)S(1)} %select_select_fusion), channel_id=1, source_target_pairs={{0,1},{1,2},{2,3},{3,4},{4,5},{5,6},{6,7},{7,0},{8,9},{9,10},{10,1... | collective-permute-start | bytes 786440 | tf_op jit(solution)/shard_map/ppermute | solution.py:12
  35.6 1.2 copy-start.6
  35.6 19.8 %copy-start.12 = (bf16[4,256,256]{2,1,0:T(8,128)(2,1)}, bf16[4,256,256]{2,1,0:T(8,128)(2,1)S(1)}, u32[]{:S(2)}) copy-start(bf16[4,256,256]{2,1,0:T(8,128)(2,1)S(1)} %get-tuple-element.422) | copy-start | bytes 1572868
  35.6 6.8 %copy-start.4 = (bf16[16,1,1,64,256]{4,3,2,1,0:T(8,128)(2,1)S(1)}, bf16[16,1,1,64,256]{4,3,2,1,0:T(8,128)(2,1)}, u32[]{:S(2)}) copy-start(bf16[16,1,1,64,256]{4,3,2,1,0:T(8,128)(2,1)} %param.23) | copy-start | bytes 1572868
  36.9 18.5 %all-to-all-start = ((bf16[4,256,256]{2,0,1:T(4,128)(2,1)}), bf16[4,256,256]{2,0,1:T(4,128)(2,1)S(1)}, u32[]{:S(2)}, u32[]{:S(2)}) async-start(bf16[4,256,256]{2,0,1:T(4,128)(2,1)} %copy.52), calls=%async_computation | async-start | bytes 1048576 | tf_op jit(solution)/shard_map/all_to_all | solution.py:149
  55.4 1.8 copy-start.9
  55.8 3.1 %copy-start.8 = (bf16[256,256]{1,0:T(8,128)(2,1)S(1)}, bf16[256,256]{1,0:T(8,128)(2,1)}, u32[]{:S(2)}) copy-start(bf16[256,256]{1,0:T(8,128)(2,1)} %param.22) | copy-start | bytes 393220
  62.3 5.0 %copy-start.5 = (bf16[16,64,4,64]{3,2,1,0:T(4,128)(2,1)S(1)}, bf16[16,64,4,64]{3,2,1,0:T(4,128)(2,1)}, u32[]{:S(2)}) copy-start(bf16[16,64,4,64]{3,2,1,0:T(4,128)(2,1)} %reshape.100) | copy-start | bytes 1572868
  67.2 5.8 %copy-start.13 = (f32[64,4,16]{2,1,0:T(4,128)}, f32[64,4,16]{2,1,0:T(4,128)S(1)}, u32[]{:S(2)}) copy-start(f32[64,4,16]{2,1,0:T(4,128)S(1)} %get-tuple-element.182) | copy-start | bytes 49156
  79.2 3.5 %copy-start.7 = (bf16[16,64,4,64]{3,0,2,1:T(8,128)(2,1)S(1)}, bf16[16,64,4,64]{3,0,2,1:T(8,128)(2,1)}, u32[]{:S(2)}) copy-start(bf16[16,64,4,64]{3,0,2,1:T(8,128)(2,1)} %fusion.50) | copy-start | bytes 1572868
  92.7 1.5 copy-start.10
  95.6 16.5 %all-to-all-start.1 = ((bf16[16,64,256]{2,1,0:T(8,128)(2,1)}), bf16[16,64,256]{2,1,0:T(8,128)(2,1)S(1)}, u32[]{:S(2)}, u32[]{:S(2)}) async-start(bf16[16,64,256]{2,1,0:T(8,128)(2,1)} %bitcast.30), calls=%async_computation.1 | async-start | bytes 1048576 | tf_op jit(solution)/shard_map/all_to_all | solution.py:152
  99.1 164.7 %all-reduce.3.cloned.1.call-start = ((), (), s32[]{:S(2)}) async-start(), calls=%async_computation.2 | async-start | bytes 2097152 | tf_op jit(solution)/shard_map/psum | solution.py:168
  113.2 2.6 copy-start.3
  117.8 2.6 copy-start.3
  122.5 2.6 copy-start.3
  127.1 2.6 copy-start.3
  131.8 4.3 %copy-start.11 = (s32[4,128]{1,0:T(4,128)S(1)}, s32[4,128]{1,0:T(4,128)}, u32[]{:S(2)}) copy-start(s32[4,128]{1,0:T(4,128)} %param.17) | copy-start | bytes 6148
  131.8 4.3 %collective-permute-start.1 = (bf16[4,128,256]{2,1,0:T(8,128)(2,1)}, bf16[4,128,256]{2,1,0:T(8,128)(2,1)}, u32[]{:S(2)}, u32[]{:S(2)}) collective-permute-start(bf16[4,128,256]{2,1,0:T(8,128)(2,1)} %get-tuple-element.126), channel_id=1, source_target_pairs={{0,7},{1,0},{2,1},{3,2},{4,3},{5,4},{6,5},{7,6},{8,15},{9,8},{10,9... | collective-permute-start | bytes 786440 | tf_op jit(solution)/shard_map/ppermute | solution.py:12
Sparse Core Ops, SparseCore 0:
  133.8 129.9 all-reduce.2
where the time goes:
time: 278 us; the launch traced here: 277 us
  waiting for transfers between devices  158 us (57%)
  matrix products  53.5 us (19%)
  local copies, waits for them, and re-layouts  38.3 us (14%)
  between operations  14.4 us (5%)
  starting transfers between devices  9.7 us (3%)
  other arithmetic  3.06 us (1%)
    psum x1, waiting for transfers between devices, local(): lax.psum((grad_message, attn_grads[0], attn_grads[1], attn_grads[2]), ('d...  125 us
    all_to_all x1, waiting for transfers between devices, local(): lax.all_to_all(hidden, 'day', split_axis=1, concat_axis=0, tiled=True)  12.5 us
    all_to_all x1, waiting for transfers between devices, local(): lax.all_to_all(back, 'day', split_axis=0, concat_axis=1, tiled=True)  10.9 us
    ppermute x2, waiting for transfers between devices, from_behind(): return lax.ppermute(value, axis, pairs)  9.28 us
    gather x1, local copies, waits for them, and re-layouts, local(): picked = jnp.take_along_axis(node_states, halo_rows[:, :, None], axis=1)  7 us
    unnamed x30, local copies, waits for them, and re-layouts  6.74 us
    dot_general x1, matrix products, attend(): jnp.einsum('nhts,snhd->tnhd', score_f, key_f).astype(jnp.bfloat16)  6.14 us
    dot_general x1, matrix products, attend(): jnp.einsum('nhts,tnhd->snhd', score_f, query_f).astype(jnp.bfloat16)  5.79 us
  transfers between devices with their start and end apart: 5, of which 5 were waited for; matrix products, arithmetic and copies ran while one was open for 2% of the time, Pallas kernels for 0%

commit v1 on v0

--- a/solution.py
+++ b/solution.py
@@ -149,7 +149,10 @@
     node_major = lax.all_to_all(hidden, "day", split_axis=1, concat_axis=0, tiled=True)
     upstream = cotangent.reshape(cotangent.shape[0], -1, width)
     attn_grads, back = attend(node_major, upstream, w_query, w_key, w_value)
-    back_days = lax.all_to_all(back, "day", split_axis=0, concat_axis=1, tiled=True)
+    back_days = jnp.concatenate(
+        lax.all_to_all(jnp.stack(jnp.split(back, lax.axis_size("day"), axis=0)), "day", 0, 0),
+        axis=1,
+    )
 
     def backward_one(items):
         return gnn_backward(items[0], items[1], items[2], items[3], items[4], w_message)

time: 278 us -> 279 us (level)
    unnamed x30 -> x26, local copies, waits for them, and re-layouts: 6.74 us -> 6.73 us
where the time goes in v1:
time: 279 us; the launch traced here: 278 us
  waiting for transfers between devices  158 us (57%)
  matrix products  52.5 us (19%)
  local copies, waits for them, and re-layouts  39.5 us (14%)
  between operations  14.4 us (5%)
  starting transfers between devices  9.7 us (3%)
  other arithmetic  3.92 us (1%)
    psum x1, waiting for transfers between devices, local(): lax.psum((grad_message, attn_grads[0], attn_grads[1], attn_grads[2]), ('d...  125 us
    all_to_all x1, waiting for transfers between devices, local(): lax.all_to_all(hidden, 'day', split_axis=1, concat_axis=0, tiled=True)  12.5 us
    all_to_all x1, waiting for transfers between devices, local(): lax.all_to_all(jnp.stack(jnp.split(back, lax.axis_size('day'), axis=0)),...  10.9 us
    ppermute x2, waiting for transfers between devices, from_behind(): return lax.ppermute(value, axis, pairs)  9.29 us
    gather x1, local copies, waits for them, and re-layouts, local(): picked = jnp.take_along_axis(node_states, halo_rows[:, :, None], axis=1)  7 us
    unnamed x26, local copies, waits for them, and re-layouts  6.73 us
    dot_general x1, matrix products, attend(): jnp.einsum('nhts,tnhd->snhd', score_f, query_f).astype(jnp.bfloat16)  6.08 us
    dot_general x1, matrix products, attend(): jnp.einsum('nhts,snhd->tnhd', score_f, key_f).astype(jnp.bfloat16)  5.83 us
  transfers between devices with their start and end apart: 5, of which 5 were waited for; matrix products, arithmetic and copies ran while one was open for 2% of the time, Pallas kernels for 0%

profile of v1, /device:TPU:0, one launch (start us, length us, event | category | flops | bytes accessed | tf_op | source)
XLA Modules:
  0.0 278.3 jit_solution(8705375120052434309)
XLA Ops:
  7.2 0.7 fusion.70
  7.9 0.8 iota_compare_fusion.8
  8.7 7.0 %gather_fusion = bf16[512,256]{1,0:T(8,128)(2,1)S(1)} fusion(bf16[4,256,256]{2,1,0:T(8,128)(2,1)} %param.14, s32[512]{0:T(512)S(1)} %fusion.70), kind=kCustom, calls=%fused_computation | custom fusion | bytes 528384 | tf_op jit(solution)/shard_map/jit(take_along_axis)/gather | solution.py:137
  16.4 6.9 %collective-permute-done = bf16[4,128,256]{2,1,0:T(8,128)(2,1)S(1)} collective-permute-done((bf16[4,128,256]{2,1,0:T(8,128)(2,1)S(1)}, bf16[4,128,256]{2,1,0:T(8,128)(2,1)S(1)}, u32[]{:S(2)}, u32[]{:S(2)}) %collective-permute-start) | collective-permute-done | bytes 262176 | tf_op jit(solution)/shard_map/ppermute | solution.py:12
  23.4 12.1 %while.34 = (s32[]{:T(128)}, bf16[4,256,256]{2,1,0:T(8,128)(2,1)S(1)}, f32[4,256,256]{2,1,0:T(8,128)S(1)}, f32[4,256]{1,0:T(4,128)S(1)}, bf16[4,256,256]{2,1,0:T...) while((s32[]{:T(128)}, ...), condition=%wide.region_2.3_spmd.clone, body=%wide.region_0.2_spmd.sunk.clone | while | flops 287277312 | bytes 3111561 | solution.py:146
  23.5 0.7 constant_dynamic-slice_fusion.7
  24.2 1.0 convert_reduce_fusion.3
  25.8 0.7 bitcast_dynamic-update-slice_fusion.15
  26.5 0.7 constant_dynamic-slice_fusion.7
  27.2 1.0 convert_reduce_fusion.3
  28.8 0.7 bitcast_dynamic-update-slice_fusion.15
  29.5 0.7 constant_dynamic-slice_fusion.7
  30.3 1.0 convert_reduce_fusion.3
  31.8 0.7 bitcast_dynamic-update-slice_fusion.15
  32.6 0.7 constant_dynamic-slice_fusion.7
  33.3 1.0 convert_reduce_fusion.3
  34.9 0.7 bitcast_dynamic-update-slice_fusion.15
  35.6 1.2 copy.52
  36.8 5.6 %all-to-all-start = ((bf16[4,256,256]{2,0,1:T(4,128)(2,1)}), bf16[4,256,256]{2,0,1:T(4,128)(2,1)S(1)}, u32[]{:S(2)}, u32[]{:S(2)}) async-start(bf16[4,256,256]{2,0,1:T(4,128)(2,1)} %copy.52), calls=%async_computation | async-start | bytes 1048576 | tf_op jit(solution)/shard_map/all_to_all | solution.py:149
  42.9 12.5 %all-to-all-done = bf16[4,256,256]{2,0,1:T(4,128)(2,1)S(1)} async-done(((bf16[4,256,256]{2,0,1:T(4,128)(2,1)}), bf16[4,256,256]{2,0,1:T(4,128)(2,1)S(1)}, u32[]{:S(2)}, u32[]{:S(2)}) %all-to-all-start) | async-done | bytes 524320 | tf_op jit(solution)/shard_map/all_to_all | solution.py:149
  55.8 1.4 reshape.111
  57.5 1.4 reshape.112
  59.6 2.6 fusion.52
  62.2 4.9 %fusion.78 = (f32[64,4,16]{2,1,0:T(4,128)S(1)}, f32[64,4,16,16]{2,3,1,0:T(8,128)}) fusion(pred[16,16]{0,1:T(8,128)(4,1)S(1)} %iota_compare_fusion.7, bf16[16,64,4,64]{3,2,1,0:T(4,128)(2,1)} %reshape.111, bf16[16,64,4,64]{3,2,1,0:T(4,128)(2,1)} %reshape.112), kind=kOutput, calls=%fused_computation.121 | convolution fusion | flops 8650767 | bytes 1327360 | tf_op jit(solution)/shard_map/sub | solution.py:85
  67.1 6.1 %fusion.50 = bf16[16,64,4,64]{3,0,2,1:T(8,128)(2,1)} fusion(f32[64,4,16,16]{3,2,1,0:T(8,128)} %fusion.52, bf16[16,64,4,64]{3,2,1,0:T(4,128)(2,1)} %reshape.112, f32[64,4,16,16]{2,3,1,0:T(8,128)} %get-tuple-element.187, f32[64,4,16]{2,1,0:T(4,128)S(1)} %get-tuple-element.186), kind=kOutput, calls=%fused_computation.78 | convolution fusion | flops 9113615 | bytes 1589248 | tf_op jit(solution)/shard_map/nhts,tnhd->snhd/dot_general | solution.py:96
  73.2 5.8 %fusion.48 = bf16[16,64,4,64]{3,0,2,1:T(8,128)(2,1)} fusion(f32[64,4,16,16]{3,2,1,0:T(8,128)} %fusion.52, bf16[16,64,4,64]{3,2,1,0:T(4,128)(2,1)S(1)} %copy-done.5, f32[64,4,16,16]{2,3,1,0:T(8,128)} %get-tuple-element.187, f32[64,4,16]{2,1,0:T(4,128)S(1)} %get-tuple-element.186), kind=kOutput, calls=%fused_computation.76 | convolution fusion | flops 9113615 | bytes 1589248 | tf_op jit(solution)/shard_map/nhts,snhd->tnhd/dot_general | solution.py:95
  79.0 3.5 %fusion.49 = bf16[16,64,4,64]{3,0,2,1:T(8,128)(2,1)} fusion(bf16[16,64,4,64]{3,2,1,0:T(4,128)(2,1)S(1)} %reshape_reshape.4, f32[64,4,16,16]{2,3,1,0:T(8,128)} %get-tuple-element.187, f32[64,4,16]{2,1,0:T(4,128)S(1)} %get-tuple-element.186), kind=kOutput, calls=%fused_computation.77 | convolution fusion | flops 8781824 | bytes 1327104 | tf_op jit(solution)/shard_map/nhts,tnhd->snhd/dot_general | solution.py:89
  82.5 2.9 %copy.63 = bf16[16,64,4,64]{1,0,3,2:T(8,128)(2,1)S(1)} copy(bf16[16,64,4,64]{3,0,2,1:T(8,128)(2,1)} %fusion.50) | data formatting | bytes 1048576 | tf_op jit(solution)/shard_map/convert_element_type | solution.py:96
  85.4 0.7 reshape.115
  86.1 3.1 %copy.61 = bf16[16,64,4,64]{1,0,3,2:T(8,128)(2,1)S(1)} copy(bf16[16,64,4,64]{3,0,2,1:T(8,128)(2,1)} %fusion.48) | data formatting | bytes 1048576 | tf_op jit(solution)/shard_map/convert_element_type | solution.py:95
  89.2 0.7 reshape.114
  89.9 2.9 %copy.65 = bf16[16,64,4,64]{1,0,3,2:T(8,128)(2,1)S(1)} copy(bf16[16,64,4,64]{3,0,2,1:T(8,128)(2,1)} %fusion.49) | data formatting | bytes 1048576 | tf_op jit(solution)/shard_map/convert_element_type | solution.py:89
  92.8 0.7 reshape.116
  93.6 1.4 convolution_add_fusion.3
  95.8 0.9 pad_maximum_fusion
  96.7 3.5 %all-to-all-start.1 = ((bf16[4,4,64,256]{3,2,1,0:T(8,128)(2,1)}), bf16[4,4,64,256]{3,2,1,0:T(8,128)(2,1)S(1)}, u32[]{:S(2)}, u32[]{:S(2)}) async-start(bf16[4,4,64,256]{3,2,1,0:T(8,128)(2,1)} %pad_maximum_fusion), calls=%async_computation.1 | async-start | bytes 1048576 | tf_op jit(solution)/shard_map/all_to_all | solution.py:153
  100.2 1.1 fusion.88
  101.3 1.0 fusion.87
  102.3 10.9 %all-to-all-done.1 = bf16[4,4,64,256]{3,2,1,0:T(8,128)(2,1)S(1)} async-done(((bf16[4,4,64,256]{3,2,1,0:T(8,128)(2,1)}), bf16[4,4,64,256]{3,2,1,0:T(8,128)(2,1)S(1)}, u32[]{:S(2)}, u32[]{:S(2)}) %all-to-all-start.1) | async-done | bytes 524320 | tf_op jit(solution)/shard_map/all_to_all | solution.py:153
  113.2 0.8 copy.66
  114.2 18.6 %while.35 = (s32[]{:T(128)}, f32[4,256,256]{2,1,0:T(8,128)S(1)}, f32[4,256,256]{2,1,0:T(8,128)S(1)}, bf16[4,128,256]{2,1,0:T(8,128)(2,1)}, bf16[4,256,256]{2,1,0...) while((s32[]{:T(128)}, f32[4,256,256]{2,1,0:T(8,128)S(1)}, ...), condition=%wide.region_7.8_spmd.clone, body=%wide.region_6.7_spmd.sunk.clone | while | flops 370671616 | bytes 5576841 | solution.py:160
  114.2 1.3 convolution_multiply_fusion.3
  115.5 1.3 fusion.150
  116.9 0.6 fusion.152
  117.5 1.3 fusion.149
  118.9 1.3 convolution_multiply_fusion.3
  120.2 1.3 fusion.150
  121.5 0.6 fusion.152
  122.2 1.3 fusion.149
  123.5 1.3 convolution_multiply_fusion.3
  124.8 1.3 fusion.150
  126.9 1.3 fusion.149
  128.2 1.3 convolution_multiply_fusion.3
  129.5 1.3 fusion.150
  131.5 1.3 fusion.149
  132.9 1.0 fusion.89
  133.9 0.8 reduce_sum.38
  134.7 2.4 collective-permute-done.1
  137.1 2.4 convolution_add_fusion.4
  139.5 125.3 %all-reduce.3.cloned.1.call-done = (f32[256,256]{1,0:T(8,128)}, f32[256,256]{1,0:T(8,128)}, f32[256,256]{1,0:T(8,128)}, f32[256,256]{1,0:T(8,128)}) async-done(((f32[256,256]{1,0:T(8,128)}, f32[256,256]{1,0:T(8,128)}, f32[256,256]{1,0:T(8,128)}, f32[256,256]{1,0:T(8,128)}), (f32[256,256]{1,0:T(8,128)}, f32[256,256]{1,0:T(8,128)}, f32[256,256]{1,0:T(8,128)}, ...) | async-done | bytes 1048592 | tf_op jit(solution)/shard_map/psum | solution.py:171
  264.8 1.7 copy.137
  266.5 1.7 copy.138
  268.1 1.7 copy.139
  269.8 1.7 copy.140
  (92 shorter events, 7.5 us)
Async XLA Ops:
  7.2 50.0 %copy-start = (bf16[256,256]{1,0:T(8,128)(2,1)S(1)}, bf16[256,256]{1,0:T(8,128)(2,1)}, u32[]{:S(2)}) copy-start(bf16[256,256]{1,0:T(8,128)(2,1)} %param.20) | copy-start | bytes 393220
  8.7 14.8 %copy-start.1 = (bf16[4,256,256]{2,1,0:T(8,128)(2,1)S(1)}, bf16[4,256,256]{2,1,0:T(8,128)(2,1)}, u32[]{:S(2)}) copy-start(bf16[4,256,256]{2,1,0:T(8,128)(2,1)} %param.14) | copy-start | bytes 1572868
  8.7 14.8 %copy-start.2 = (bf16[256,256]{1,0:T(8,128)(2,1)S(1)}, bf16[256,256]{1,0:T(8,128)(2,1)}, u32[]{:S(2)}) copy-start(bf16[256,256]{1,0:T(8,128)(2,1)} %param.19) | copy-start | bytes 393220
  15.9 7.4 %collective-permute-start = (bf16[4,128,256]{2,1,0:T(8,128)(2,1)S(1)}, bf16[4,128,256]{2,1,0:T(8,128)(2,1)S(1)}, u32[]{:S(2)}, u32[]{:S(2)}) collective-permute-start(bf16[4,128,256]{2,1,0:T(8,128)(2,1)S(1)} %select_select_fusion), channel_id=1, source_target_pairs={{0,1},{1,2},{2,3},{3,4},{4,5},{5,6},{6,7},{7,0},{8,9},{9,10},{10,1... | collective-permute-start | bytes 786440 | tf_op jit(solution)/shard_map/ppermute | solution.py:12
  35.6 1.2 copy-start.6
  35.6 19.8 %copy-start.11 = (bf16[4,256,256]{2,1,0:T(8,128)(2,1)}, bf16[4,256,256]{2,1,0:T(8,128)(2,1)S(1)}, u32[]{:S(2)}) copy-start(bf16[4,256,256]{2,1,0:T(8,128)(2,1)S(1)} %get-tuple-element.426) | copy-start | bytes 1572868
  35.6 6.8 %copy-start.4 = (bf16[16,1,1,64,256]{4,3,2,1,0:T(8,128)(2,1)S(1)}, bf16[16,1,1,64,256]{4,3,2,1,0:T(8,128)(2,1)}, u32[]{:S(2)}) copy-start(bf16[16,1,1,64,256]{4,3,2,1,0:T(8,128)(2,1)} %param.23) | copy-start | bytes 1572868
  36.8 18.5 %all-to-all-start = ((bf16[4,256,256]{2,0,1:T(4,128)(2,1)}), bf16[4,256,256]{2,0,1:T(4,128)(2,1)S(1)}, u32[]{:S(2)}, u32[]{:S(2)}) async-start(bf16[4,256,256]{2,0,1:T(4,128)(2,1)} %copy.52), calls=%async_computation | async-start | bytes 1048576 | tf_op jit(solution)/shard_map/all_to_all | solution.py:149
  42.5 13.0 %copy-start.8 = (bf16[256,256]{1,0:T(8,128)(2,1)S(1)}, bf16[256,256]{1,0:T(8,128)(2,1)}, u32[]{:S(2)}) copy-start(bf16[256,256]{1,0:T(8,128)(2,1)} %param.21) | copy-start | bytes 393220
  55.8 3.1 %copy-start.7 = (bf16[256,256]{1,0:T(8,128)(2,1)S(1)}, bf16[256,256]{1,0:T(8,128)(2,1)}, u32[]{:S(2)}) copy-start(bf16[256,256]{1,0:T(8,128)(2,1)} %param.22) | copy-start | bytes 393220
  67.1 6.1 %copy-start.5 = (bf16[16,64,4,64]{3,2,1,0:T(4,128)(2,1)S(1)}, bf16[16,64,4,64]{3,2,1,0:T(4,128)(2,1)}, u32[]{:S(2)}) copy-start(bf16[16,64,4,64]{3,2,1,0:T(4,128)(2,1)} %reshape.111) | copy-start | bytes 1572868
  93.6 1.5 copy-start.9
  96.7 16.5 %all-to-all-start.1 = ((bf16[4,4,64,256]{3,2,1,0:T(8,128)(2,1)}), bf16[4,4,64,256]{3,2,1,0:T(8,128)(2,1)S(1)}, u32[]{:S(2)}, u32[]{:S(2)}) async-start(bf16[4,4,64,256]{3,2,1,0:T(8,128)(2,1)} %pad_maximum_fusion), calls=%async_computation.1 | async-start | bytes 1048576 | tf_op jit(solution)/shard_map/all_to_all | solution.py:153
  100.1 164.6 %all-reduce.3.cloned.1.call-start = ((), (), s32[]{:S(2)}) async-start(), calls=%async_computation.2 | async-start | bytes 2097152 | tf_op jit(solution)/shard_map/psum | solution.py:171
  114.2 2.6 copy-start.3
  118.9 2.6 copy-start.3
  123.5 2.6 copy-start.3
  128.2 2.6 copy-start.3
  132.8 4.3 %copy-start.10 = (s32[4,128]{1,0:T(4,128)S(1)}, s32[4,128]{1,0:T(4,128)}, u32[]{:S(2)}) copy-start(s32[4,128]{1,0:T(4,128)} %param.17) | copy-start | bytes 6148
  132.8 4.3 %collective-permute-start.1 = (bf16[4,128,256]{2,1,0:T(8,128)(2,1)}, bf16[4,128,256]{2,1,0:T(8,128)(2,1)}, u32[]{:S(2)}, u32[]{:S(2)}) collective-permute-start(bf16[4,128,256]{2,1,0:T(8,128)(2,1)} %get-tuple-element.126), channel_id=1, source_target_pairs={{0,7},{1,0},{2,1},{3,2},{4,3},{5,4},{6,5},{7,6},{8,15},{9,8},{10,9... | collective-permute-start | bytes 786440 | tf_op jit(solution)/shard_map/ppermute | solution.py:12
Sparse Core Ops, SparseCore 0:
  134.9 129.8 all-reduce.2
